TPU v7x, 32 devices: a whole 2x2x4 slice. The times are simulated.
32 devices in a mesh: dp: 4 (over x, core), label: 8 (over z, y).
Axes of the slice: x: 2, y: 2, z: 4, core: 2. Of those that a mesh axis runs over, the one named last changes fastest.
Arguments:
- token_ids: int32 [64, 2, 32], P(('dp', 'label')), may hold values from 0 to 4095
- labeled: int32 [64], P(('dp', 'label')), may hold values from 0 to 1, as said below
- positive_ids: int32 [64, 16], P(('dp', 'label')), may hold values from 0 to 163839
- vocab_table: bfloat16 [4096, 768], P(('dp', 'label')), may hold values from -6 to 6
- enc_weight: bfloat16 [768, 768], replicated, may hold values from -0.21875 to 0.21875
- label_matrix: bfloat16 [163840, 768], P(('dp', 'label')), may hold values from -0.21875 to 0.21875
- label_log_rates: float32 [163840], P(('dp', 'label')), may hold values from -11.5 to -6.9
Outputs:
- loss: float32 [], replicated
- grad_weight: float32 [768, 768], replicated
- new_log_rates: float32 [163840], P(('dp', 'label'))
Inputs may be any that keep to these rules, and one draw needn't show every extreme that they name: At least one document has labeled = 1.
All inputs are finite; a program needn't handle non-finite values.
Results may differ from a plain program's by a relative error of at most 0.0042.
Values may be sent and summed in bfloat16 or wider, within the bound.
No kernel may reach another device: no remote copies, remote signals or barrier semaphores. Data moves between devices by JAX's collectives and lax.ppermute only.
A program may use at most 128 MiB of HBM per device.

v0:
```python
import jax
import jax.numpy as jnp
from jax import lax
from jax.sharding import PartitionSpec as P


def encode(pooled_rows, enc_weight):
    pre = jnp.dot(pooled_rows, enc_weight, preferred_element_type=jnp.float32)
    inv_norm = lax.rsqrt(jnp.sum(pre * pre, axis=-1, keepdims=True) + 1e-06)
    return (pre * inv_norm, inv_norm)


def tangent(grad_emb, unit_strong, inv_strong):
    return (
        grad_emb - unit_strong * jnp.sum(unit_strong * grad_emb, axis=-1, keepdims=True)
    ) * inv_strong


def outer_sum(pooled_strong, grad_pre):
    return jnp.einsum("dk,dj->kj", pooled_strong, grad_pre, precision=lax.Precision.HIGHEST)


def shards(
    token_ids, labeled, positive_ids, vocab_table, enc_weight, label_matrix, label_log_rates
):
    own_docs = token_ids.shape[0]
    title = token_ids.shape[2]
    width = vocab_table.shape[1]
    vocab_rows = vocab_table.shape[0]
    label_rows = label_matrix.shape[0]
    shard_index = lax.axis_index(("dp", "label"))
    all_tokens, all_labeled, all_positives = (
        lax.all_gather(token_ids, ("dp", "label"), axis=0, tiled=True),
        lax.all_gather(labeled, ("dp", "label"), axis=0, tiled=True),
        lax.all_gather(positive_ids, ("dp", "label"), axis=0, tiled=True),
    )
    docs_all = all_tokens.shape[0]
    flat_tokens = all_tokens.reshape(docs_all * 2, title)
    local_ids = flat_tokens - shard_index * vocab_rows
    vocab_codes = jnp.arange(vocab_rows, dtype=jnp.int32)
    rows = local_ids
    tally = jnp.zeros((lax.axis_size(("dp", "label")) * (own_docs * 2), vocab_rows), jnp.float32)
    for position in range(title):
        tally = tally + (rows[:, position : position + 1] == vocab_codes[None, :]).astype(
            jnp.float32
        )
    pooled_rows = lax.psum_scatter(
        jnp.dot(tally.astype(jnp.bfloat16), vocab_table, preferred_element_type=jnp.float32)
        * (1.0 / title),
        ("dp", "label"),
        scatter_dimension=0,
        tiled=True,
    ).astype(jnp.bfloat16)
    pooled_own = jnp.transpose(pooled_rows.reshape(own_docs, 2, width), (1, 0, 2))
    unit_own, inv_own = encode(pooled_own.reshape(2 * own_docs, width), enc_weight)
    emb_own = unit_own.astype(jnp.bfloat16).reshape(2, own_docs, width)
    scores = (
        jnp.einsum(
            "vrk,lk->vrl",
            lax.all_gather(emb_own, ("dp", "label"), axis=1, tiled=True),
            label_matrix,
            preferred_element_type=jnp.float32,
        )
        * 16.0
        - 6.0
    )
    weak = scores[0]
    strong = scores[1]
    teacher = jax.nn.sigmoid(weak)
    mean_teacher = jnp.mean(teacher, axis=0)
    label_codes = shard_index * label_rows + jnp.arange(label_rows, dtype=jnp.int32)
    hit = jnp.zeros((docs_all, label_rows), dtype=bool)
    for column in range(all_positives.shape[1]):
        hit = hit | (all_positives[:, column : column + 1] == label_codes[None, :])
    flag = (all_labeled == 1)[:, None]
    rates = jnp.exp(label_log_rates)
    target = jnp.where(
        flag, hit.astype(jnp.float32), teacher * rates[None, :] / mean_teacher[None, :]
    )
    total_local = jnp.sum(target)
    loss_local = jnp.sum(jax.nn.softplus(strong) - target * strong)
    slope = (jax.nn.sigmoid(strong) - target).astype(jnp.bfloat16)
    labeled_count = jnp.sum(all_labeled).astype(jnp.float32)
    batch_rate = jnp.sum((flag & hit).astype(jnp.float32), axis=0) / labeled_count
    new_log_rates = jnp.log(0.9 * rates + 0.1 * batch_rate)
    factor = jnp.float32(16.0)
    rows = slope
    grad_emb = lax.psum_scatter(
        jnp.dot(rows, label_matrix, preferred_element_type=jnp.float32) * factor,
        ("dp", "label"),
        scatter_dimension=0,
        tiled=True,
    )
    grad_pre = tangent(grad_emb, unit_own[own_docs:], inv_own[own_docs:])
    weight_local = outer_sum(pooled_own[1].astype(jnp.float32), grad_pre)
    weight_sum, total, loss_sum = lax.psum((weight_local, total_local, loss_local), ("dp", "label"))
    grad_weight = weight_sum / total
    loss = loss_sum / total
    return (loss, grad_weight, new_log_rates)


def solution(mesh):
    return jax.shard_map(
        shards,
        mesh=mesh,
        in_specs=(
            P(("dp", "label"), None, None),
            P(("dp", "label")),
            P(("dp", "label"), None),
            P(("dp", "label"), None),
            P(),
            P(("dp", "label"), None),
            P(("dp", "label")),
        ),
        out_specs=(P(), P(), P(("dp", "label"))),
        check_vma=False,
    )
```

profile of v0, /device:TPU:0, one launch (start us, length us, event | category | flops | bytes accessed | tf_op | source)
XLA Modules:
  0.0 601.3 jit_solution(3730162300531680459)
XLA Ops:
  7.2 0.9 dynamic-update-slice
  8.2 42.0 %all-reduce = s32[64]{0:T(128)S(1)} all-reduce(s32[64]{0:T(128)S(1)} %dynamic-update-slice), channel_id=1, replica_groups=mesh['dp'=4,'label'=8] {'dp','label'}, use_global_device_ids=true, to_apply=%add | all-reduce | flops 64 | bytes 512
  51.3 66.4 %all_gather.12 = s32[64,2,32]{2,1,0:T(2,128)S(1)} all-gather(s32[2,2,32]{2,1,0:T(2,128)} %param.7), channel_id=1, replica_groups=mesh['dp'=4,'label'=8] {'dp','label'}, dimensions={0}, use_global_device_ids=true | all-gather | bytes 16896 | tf_op jit(solution)/shard_map/all_gather | solution.py:33
  119.1 63.5 %all-gather = s32[32,2,16]{2,1,0:T(2,128)S(1)} all-gather(s32[1,2,16]{2,1,0:T(2,128)S(1)} %bitcast.122), channel_id=1, replica_groups=mesh['dp'=4,'label'=8] {'dp','label'}, dimensions={0}, use_global_device_ids=true | all-gather | bytes 4224 | tf_op jit(solution)/shard_map/all_gather | solution.py:35
  182.6 0.8 fusion.65
  184.2 0.8 copy.204
  185.1 0.8 copy.203
  185.9 0.8 copy.202
  186.8 0.8 copy.201
  187.6 0.8 copy.200
  189.3 1.4 copy.198
  190.6 1.3 copy.197
  196.5 43.1 %all-reduce.11 = bf16[128,768]{1,0:T(8,128)(2,1)S(1)} all-reduce(f32[128,768]{1,0:T(8,128)S(1)} %convolution_multiply_fusion), channel_id=2, replica_groups=mesh['dp'=4,'label'=8] {'dp','label'}, use_global_device_ids=true, to_apply=%region_0.0.clone | all-reduce | flops 98304 | bytes 589824
  240.2 65.1 %all_gather.13 = bf16[2,64,768]{2,0,1:T(2,128)(2,1)S(1)} all-gather(bf16[2,2,768]{2,0,1:T(2,128)(2,1)S(1)} %copy.140), channel_id=1, replica_groups=mesh['dp'=4,'label'=8] {'dp','label'}, dimensions={1}, use_global_device_ids=true | all-gather | bytes 202752 | tf_op jit(solution)/shard_map/all_gather | solution.py:60
  305.3 5.9 fusion.5
  311.9 2.7 convert_reduce_fusion
  315.3 3.4 fusion.60
  318.6 5.5 convolution_multiply_fusion.1
  324.2 122.2 %all-reduce.10.cloned.1.call-done = f32[64,768]{1,0:T(8,128)} async-done(((f32[64,768]{1,0:T(8,128)}), f32[64,768]{1,0:T(8,128)}) %all-reduce.10.cloned.1.call-update) | async-done | bytes 196624
  446.4 0.9 multiply_reduce_fusion.1
  447.3 3.3 fusion.50
  450.6 41.7 %all-reduce.3 = (f32[]{:T(128)}, f32[]{:T(128)}) all-reduce(f32[]{:T(128)} %get-tuple-element.4, f32[]{:T(128)} %get-tuple-element.3), channel_id=1, replica_groups=mesh['dp'=4,'label'=8] {'dp','label'}, use_global_device_ids=true, to_apply=%region_4.5 | all-reduce | flops 2 | bytes 16 | tf_op jit(solution)/shard_map/psum | solution.py:96
  493.6 95.9 %all-reduce.8.cloned.1.call-done = f32[768,768]{1,0:T(8,128)} async-done(((f32[768,768]{1,0:T(8,128)}), f32[768,768]{1,0:T(8,128)}) %all-reduce.8.cloned.1.call-update) | async-done | bytes 2359312 | tf_op jit(solution)/shard_map/psum | solution.py:96
  589.5 3.9 broadcast_divide_fusion
  (82 shorter events, 10.0 us)
Async XLA Ops:
  7.2 232.5 %copy-start = (bf16[768,768]{1,0:T(8,128)(2,1)S(1)}, bf16[768,768]{1,0:T(8,128)(2,1)}, u32[]{:S(2)}) copy-start(bf16[768,768]{1,0:T(8,128)(2,1)} %param.11) | copy-start | bytes 3538948
  7.2 439.2 %all-reduce.10.cloned.1.call-start = ((), (), s32[]{:S(2)}) async-start(), calls=%async_computation.1 | async-start | bytes 393216
  118.0 1.1 copy-start.6
  193.0 2.6 copy-start.7
  311.2 0.7 copy-start.2
  311.2 0.7 copy-start.3
  311.2 0.7 copy-start.4
  311.2 0.7 copy-start.5
  311.2 3.4 copy-start.1
  324.1 265.4 %all-reduce.8.cloned.1.call-start = ((), (), s32[]{:S(2)}) async-start(), calls=%async_computation | async-start | bytes 4718592 | tf_op jit(solution)/shard_map/psum | solution.py:96
Sparse Core Ops, SparseCore 0:
  324.2 122.1 all-reduce.9
  452.5 136.9 all-reduce.7
where the time goes:
time: 603 us; the launch traced here: 601 us
  blocking collectives  322 us (53%)
  waiting for transfers between devices  218 us (36%)
  between operations  17.4 us (3%)
  matrix products  15.8 us (3%)
  local copies, waits for them, and re-layouts  15.1 us (3%)
  other arithmetic  13 us (2%)
    unnamed x3, waiting for transfers between devices  122 us
    psum x1, waiting for transfers between devices, shards(): lax.psum((weight_local, total_local, loss_local), ('dp', 'label'))  95.9 us
    unnamed x2, blocking collectives  85 us
    all_gather x1, blocking collectives, shards(): lax.all_gather(token_ids, ('dp', 'label'), axis=0, tiled=True)  66.4 us
    all_gather x1, blocking collectives, shards(): lax.all_gather(emb_own, ('dp', 'label'), axis=1, tiled=True)  65.1 us
    all_gather x1, blocking collectives, shards(): lax.all_gather(positive_ids, ('dp', 'label'), axis=0, tiled=True)  63.5 us
    psum x1, blocking collectives, shards(): lax.psum((weight_local, total_local, loss_local), ('dp', 'label'))  41.7 us
    unnamed x66, local copies, waits for them, and re-layouts  13.5 us
  transfers between devices with their start and end apart: 2, of which 2 were waited for; matrix products, arithmetic and copies ran while one was open for 0% of the time, Pallas kernels for 0%

commit v1 on v0

--- a/solution.py
+++ b/solution.py
@@ -1,7 +1,38 @@
+import functools
 import jax
 import jax.numpy as jnp
 from jax import lax
 from jax.sharding import PartitionSpec as P
+
+
+def begin_roads(panel, on_dim):
+    panel = jnp.moveaxis(panel, 0, on_dim)
+    main = panel.shape
+    tmp = panel.reshape(*main[:on_dim], main[on_dim] * main[on_dim + 1], *main[on_dim + 2 :])
+    return tmp
+
+
+def _serve_map(local_array, a_name):
+    world = lax.psum(1, axis_name=a_name)
+    all_values = local_array[None]
+    for pp in range(world.bit_length() - 1):
+        field_out = 1 << pp
+        y2 = lax.ppermute(
+            all_values, axis_name=a_name, perm=[(b, b ^ field_out) for b in range(world)]
+        )
+        heard = jnp.stack([all_values, y2], 0)
+        far_arr = lax.axis_index(a_name)
+        w2 = far_arr >> pp & 1
+        all_values = jnp.where(w2 == 0, heard, heard[::-1]).reshape(-1, *local_array.shape)
+    return all_values
+
+
+def push_the_core(shard_in, local_block, dim_at):
+    next_value = begin_roads(_serve_map(shard_in, local_block), dim_at)
+    return next_value
+
+
+fit_blocks_all = functools.partial(push_the_core, local_block=("dp", "label"), dim_at=1)
 
 
 def encode(pooled_rows, enc_weight):
@@ -56,10 +87,7 @@
     emb_own = unit_own.astype(jnp.bfloat16).reshape(2, own_docs, width)
     scores = (
         jnp.einsum(
-            "vrk,lk->vrl",
-            lax.all_gather(emb_own, ("dp", "label"), axis=1, tiled=True),
-            label_matrix,
-            preferred_element_type=jnp.float32,
+            "vrk,lk->vrl", fit_blocks_all(emb_own), label_matrix, preferred_element_type=jnp.float32
         )
         * 16.0
         - 6.0

time: 603 us -> 543 us (0.900)
  blocking collectives: 322 us -> 255 us
  local copies, waits for them, and re-layouts: 15.1 us -> 5.13 us
  starting transfers between devices: 0.08 us -> 8.98 us
  waiting for transfers between devices: 218 us -> 226 us
    all_gather x1 -> x0, blocking collectives: 65.1 us -> none  [shards(): lax.all_gather(emb_own, ('dp', 'label'), axis=1, tiled=True)]
    unnamed x66 -> x60, local copies, waits for them, and re-layouts: 13.5 us -> 3.98 us
    ppermute x0 -> x5, starting transfers between devices: none -> 8.9 us  [_serve_map(): lax.ppermute(all_values, axis_name=a_name, perm=[(b, b ^ field_out) for b...]
    unnamed x2, blocking collectives: 85 us -> 78.9 us
  transfers between devices with their start and end apart: 2 -> 7, of which waited for: 2 -> 5; matrix products, arithmetic and copies ran while one was open for 0% -> 1% of each run, Pallas kernels for 0% -> 0%
where the time goes in v1:
time: 543 us; the launch traced here: 542 us
  blocking collectives  255 us (47%)
  waiting for transfers between devices  226 us (42%)
  between operations  17.6 us (3%)
  matrix products  15.8 us (3%)
  other arithmetic  13.4 us (2%)
  starting transfers between devices  8.98 us (2%)
    unnamed x3, waiting for transfers between devices  125 us
    psum x1, waiting for transfers between devices, shards(): lax.psum((weight_local, total_local, loss_local), ('dp', 'label'))  95.8 us
    unnamed x2, blocking collectives  78.9 us
    all_gather x1, blocking collectives, shards(): lax.all_gather(token_ids, ('dp', 'label'), axis=0, tiled=True)  70.4 us
    all_gather x1, blocking collectives, shards(): lax.all_gather(positive_ids, ('dp', 'label'), axis=0, tiled=True)  64.1 us
    psum x1, blocking collectives, shards(): lax.psum((weight_local, total_local, loss_local), ('dp', 'label'))  41.7 us
  transfers between devices with their start and end apart: 7, of which 5 were waited for; matrix products, arithmetic and copies ran while one was open for 1% of the time, Pallas kernels for 0%

profile of v1, /device:TPU:0, one launch (start us, length us, event | category | flops | bytes accessed | tf_op | source)
XLA Modules:
  0.0 542.2 jit_solution(17520291304486819196)
XLA Ops:
  7.2 70.4 %all_gather.9 = s32[64,2,32]{2,1,0:T(2,128)S(1)} all-gather(s32[2,2,32]{2,1,0:T(2,128)} %param.7), channel_id=1, replica_groups=mesh['dp'=4,'label'=8] {'dp','label'}, dimensions={0}, use_global_device_ids=true | all-gather | bytes 16896 | tf_op jit(solution)/shard_map/all_gather | solution.py:64
  80.9 0.8 convolution_multiply_fusion
  81.7 41.6 %all-reduce.11 = bf16[128,768]{1,0:T(8,128)(2,1)S(1)} all-reduce(f32[128,768]{1,0:T(8,128)S(1)} %convolution_multiply_fusion), channel_id=2, replica_groups=mesh['dp'=4,'label'=8] {'dp','label'}, use_global_device_ids=true, to_apply=%region_0.0.clone | all-reduce | flops 98304 | bytes 589824
  123.9 1.4 collective-permute-start
  125.3 64.1 %all-gather = s32[32,2,16]{2,1,0:T(2,128)S(1)} all-gather(s32[1,2,16]{2,1,0:T(2,128)S(1)} %bitcast.153), channel_id=1, replica_groups=mesh['dp'=4,'label'=8] {'dp','label'}, dimensions={0}, use_global_device_ids=true | all-gather | bytes 4224 | tf_op jit(solution)/shard_map/all_gather | solution.py:66
  189.9 37.4 %all-reduce = s32[64]{0:T(128)S(1)} all-reduce(s32[64]{0:T(128)S(1)} %dynamic-update-slice), channel_id=1, replica_groups=mesh['dp'=4,'label'=8] {'dp','label'}, use_global_device_ids=true, to_apply=%add | all-reduce | flops 64 | bytes 512
  227.3 2.9 collective-permute-start.1
  230.2 1.7 collective-permute-done.1
  232.0 2.2 collective-permute-start.2
  235.4 1.4 collective-permute-done.2
  237.0 2.7 convert_reduce_fusion
  239.7 0.6 reduce_sum.69
  241.3 2.3 collective-permute-start.4
  243.7 0.6 add_log_fusion
  244.3 2.8 collective-permute-done.4
  247.6 5.9 %fusion.5 = f32[2,64,5120]{2,1,0:T(8,128)S(1)} fusion(bf16[2,64,768]{2,1,0:T(8,128)(2,1)S(1)} %reshape.73, bf16[5120,768]{1,0:T(8,128)(2,1)} %param.12), kind=kOutput, calls=%fused_computation.3 | convolution fusion | flops 1007943680 | bytes 10682368 | tf_op jit(solution)/shard_map/vrk,lk->vrl/dot_general | solution.py:89
  253.9 3.4 fusion.61
  257.3 5.5 %convolution_multiply_fusion.1 = f32[64,768]{1,0:T(8,128)} fusion(bf16[5120,768]{1,0:T(8,128)(2,1)} %param.12, f32[64,5120]{1,0:T(8,128)S(1)} %get-tuple-element.7, f32[2,64,5120]{2,1,0:T(8,128)S(1)} %fusion.5), kind=kOutput, calls=%fused_computation.20 | convolution fusion | flops 505004032 | bytes 10682368 | tf_op jit(solution)/shard_map/dot_general | solution.py:117
  262.9 124.5 %all-reduce.10.cloned.1.call-done = f32[64,768]{1,0:T(8,128)} async-done(((f32[64,768]{1,0:T(8,128)}), f32[64,768]{1,0:T(8,128)}) %all-reduce.10.cloned.1.call-update) | async-done | bytes 196624
  387.4 0.9 multiply_reduce_fusion.1
  388.2 3.3 fusion.49
  391.5 41.7 %all-reduce.3 = (f32[]{:T(128)}, f32[]{:T(128)}) all-reduce(f32[]{:T(128)} %get-tuple-element.4, f32[]{:T(128)} %get-tuple-element.3), channel_id=1, replica_groups=mesh['dp'=4,'label'=8] {'dp','label'}, use_global_device_ids=true, to_apply=%region_4.5 | all-reduce | flops 2 | bytes 16 | tf_op jit(solution)/shard_map/psum | solution.py:124
  434.5 95.8 %all-reduce.8.cloned.1.call-done = f32[768,768]{1,0:T(8,128)} async-done(((f32[768,768]{1,0:T(8,128)}), f32[768,768]{1,0:T(8,128)}) %all-reduce.8.cloned.1.call-update) | async-done | bytes 2359312 | tf_op jit(solution)/shard_map/psum | solution.py:124
  530.4 3.9 broadcast_divide_fusion
  (97 shorter events, 7.1 us)
Async XLA Ops:
  7.2 116.2 %copy-start = (bf16[768,768]{1,0:T(8,128)(2,1)S(1)}, bf16[768,768]{1,0:T(8,128)(2,1)}, u32[]{:S(2)}) copy-start(bf16[768,768]{1,0:T(8,128)(2,1)} %param.11) | copy-start | bytes 3538948
  7.2 380.2 %all-reduce.10.cloned.1.call-start = ((), (), s32[]{:S(2)}) async-start(), calls=%async_computation.1 | async-start | bytes 393216
  78.3 2.6 copy-start.3
  81.7 43.6 %copy-start.2 = (s32[2,16]{1,0:T(2,128)S(1)}, s32[2,16]{1,0:T(2,128)}, u32[]{:S(2)}) copy-start(s32[2,16]{1,0:T(2,128)} %param.9) | copy-start | bytes 388
  123.3 66.4 %copy-start.4 = (s32[2]{0:T(128)S(1)}, s32[2]{0:T(128)}, u32[]{:S(2)}) copy-start(s32[2]{0:T(128)} %param.8) | copy-start | bytes 28
  123.9 103.4 %collective-permute-start = (bf16[1,2,2,768]{3,2,1,0:T(2,128)(2,1)S(1)}, bf16[1,2,2,768]{3,2,1,0:T(2,128)(2,1)S(1)}, u32[]{:S(2)}, u32[]{:S(2)}) collective-permute-start(bf16[1,2,2,768]{3,2,1,0:T(2,128)(2,1)S(1)} %broadcast_in_dim_reshape.3), channel_id=1, source_target_pairs={{0,1},{1,0},{2,3},{3,2},{4,5},{5,4},{6,7},{7,6},{8,9},{9,8},{10,11... | collective-permute-start | bytes 18440 | tf_op jit(solution)/shard_map/ppermute | solution.py:20
  189.4 54.3 %copy-start.1 = (f32[5120]{0:T(1024)S(1)}, f32[5120]{0:T(1024)}, u32[]{:S(2)}) copy-start(f32[5120]{0:T(1024)} %param.13) | copy-start | bytes 61444
  227.3 4.6 collective-permute-start.1
  232.0 4.8 collective-permute-start.2
  236.9 4.1 collective-permute-start.3
  241.3 5.8 %collective-permute-start.4 = (bf16[16,2,2,768]{3,2,0,1:T(2,128)(2,1)S(1)}, bf16[16,2,2,768]{3,2,0,1:T(2,128)(2,1)S(1)}, u32[]{:S(2)}, u32[]{:S(2)}) collective-permute-start(bf16[16,2,2,768]{3,2,0,1:T(2,128)(2,1)S(1)} %bitcast.107), channel_id=1, source_target_pairs={{0,16},{1,17},{2,18},{3,19},{4,20},{5,21},{6,22},{7,23},{8,24},{9,... | collective-permute-start | bytes 294920 | tf_op jit(solution)/shard_map/ppermute | solution.py:20
  262.8 267.6 %all-reduce.8.cloned.1.call-start = ((), (), s32[]{:S(2)}) async-start(), calls=%async_computation | async-start | bytes 4718592 | tf_op jit(solution)/shard_map/psum | solution.py:124
Sparse Core Ops, SparseCore 0:
  262.9 124.4 all-reduce.9
  393.5 136.8 all-reduce.7
